TPU v7x, 32 devices: a whole 2x2x4 slice. The times are simulated.
32 devices in a mesh: groups: 2 (over y), feat: 4 (over z), tower: 4 (over x, core).
Axes of the slice: x: 2, y: 2, z: 4, core: 2. Of those that a mesh axis runs over, the one named last changes fastest.
Arguments:
- pooled_first: bfloat16 [4, 16, 3072, 128], P('tower', 'feat', 'groups'), parts along dimension 2, may hold values from -6 to 6
- pooled_second: bfloat16 [4, 16, 3072, 128], P('tower', 'feat', 'groups'), parts along dimension 2, may hold values from -6 to 6
- feature_order: int32 [4, 32], P('tower'), may hold values from 0 to 31, each once within a row
- cross_down: bfloat16 [4, 4096, 256], P('tower', 'feat'), may hold values from -0.09375 to 0.09375
- cross_up: bfloat16 [4, 4096, 256], P('tower', 'feat'), may hold values from -0.375 to 0.375
- cross_bias: float32 [4, 4096], P('tower'), may hold values from -3 to 3
- compress_weight: bfloat16 [4, 4096, 512], P('tower', 'feat'), may hold values from -0.09375 to 0.09375
- compress_bias: float32 [4, 512], P('tower'), may hold values from -3 to 3
- dense_vector: bfloat16 [3072, 128], P(('groups', 'feat', 'tower')), parts along dimension 0, may hold values from -6 to 6
- mlp_weight: bfloat16 [248, 1024], P('tower'), may hold values from -0.375 to 0.375
- mlp_bias: float32 [1024], replicated, may hold values from -3 to 3
Outputs:
- top_hidden: bfloat16 [3072, 1024], P(('groups', 'feat', 'tower')), parts along dimension 0
There are 2 independent parts, one for each index of `groups`. A program takes and returns all parts, laid end to end along the dimension named above; an argument that names none is the same for every part. Nothing has to cross between parts.
Inputs may be any that keep to these rules, and one draw needn't show every extreme that they name: Each row of feature_order names every number from 0 to 31 once.
All inputs are finite; a program needn't handle non-finite values.
Results may differ from a plain program's by a relative error of at most 0.0072.
Values may be sent and summed in bfloat16 or wider, within the bound.
No kernel may reach another device: no remote copies, remote signals or barrier semaphores. Data moves between devices by JAX's collectives and lax.ppermute only.
A program may use at most 64 MiB of HBM per device.

v0:
```python
import functools
import math
import jax
import jax.numpy as jnp
import numpy as np
from jax import lax
from jax.sharding import PartitionSpec as P


def pair_positions(vector_count):
    upper_rows, upper_cols = np.triu_indices(vector_count, 1)
    return upper_rows * vector_count + upper_cols


def received_feature_table(rows_here, feat_count, group_count, entry_count):
    piece = rows_here // group_count
    table = np.zeros((group_count, group_count, feat_count * piece // entry_count), np.int32)
    for group in range(group_count):
        for shift in range(group_count):
            source = (group - shift) % group_count
            blocks = []
            for owner in range(feat_count):
                start = owner * rows_here + source * piece
                blocks.extend(range(start // entry_count, (start + piece) // entry_count))
            table[group, shift] = blocks
    return table


def gather_rows(part, group_count):
    own = lax.all_gather(part, "feat", axis=0, tiled=True)
    received = [own]
    for shift in range(1, group_count):
        pairs = [(source, (source + shift) % group_count) for source in range(group_count)]
        received.append(lax.ppermute(own, "groups", pairs))
    return received


def on_device(
    pooled_first,
    pooled_second,
    feature_order,
    cross_down,
    cross_up,
    cross_bias,
    compress_weight,
    compress_bias,
    dense_vector,
    mlp_weight,
    mlp_bias,
    *,
    feat_count,
    group_count
):
    entry_count = pooled_first.shape[3]
    rows_here = cross_down.shape[1]
    rank = cross_down.shape[2]
    split = rows_here % group_count == 0 and rows_here // group_count % entry_count == 0
    share_count = group_count if split else 1
    piece = rows_here // share_count
    first_here = jnp.concatenate([cross_down[0], cross_up[0]], axis=1)
    second_here = compress_weight[0]
    if split:
        group_index = lax.axis_index("groups")
        first_here = lax.dynamic_slice_in_dim(first_here, group_index * piece, piece, axis=0)
        second_here = lax.dynamic_slice_in_dim(second_here, group_index * piece, piece, axis=0)
        table = jnp.asarray(received_feature_table(rows_here, feat_count, share_count, entry_count))
        position_feature = table[group_index]
    else:
        position_feature = jnp.asarray(
            received_feature_table(rows_here, feat_count, 1, entry_count)
        )[0]
    first_parts = gather_rows(first_here, share_count)
    second_parts = gather_rows(second_here, share_count)
    group_one, group_two = (
        lax.all_to_all(pooled_first, "feat", split_axis=2, concat_axis=1, tiled=True),
        lax.all_to_all(pooled_second, "feat", split_axis=2, concat_axis=1, tiled=True),
    )
    mlp_weight, group_one = lax.optimization_barrier((mlp_weight, group_one))
    hidden_weight = lax.all_gather(mlp_weight, "tower", axis=0, tiled=True)
    slot_data = jnp.concatenate([group_one[0], group_two[0]], 0)
    slot_count = slot_data.shape[0]
    row_count = slot_data.shape[1]
    orders = feature_order[0]
    position_count = position_feature.shape[1]
    one_hot = (orders[None, None, :] == position_feature[:, :, None]).astype(jnp.bfloat16)
    base_parts = jnp.einsum("kfs,sre->krfe", one_hot, slot_data, preferred_element_type=jnp.float32)
    base_parts = base_parts.astype(jnp.bfloat16).reshape(
        share_count, row_count, position_count * entry_count
    )
    bias_blocks = cross_bias[0].reshape(slot_count, entry_count)
    low_sum = None
    for shift in range(share_count):
        term = jnp.dot(
            base_parts[shift], first_parts[shift][:, :rank], preferred_element_type=jnp.float32
        )
        low_sum = term if low_sum is None else low_sum + term
    low_rank = low_sum.astype(jnp.bfloat16)
    squeezed = None
    for shift in range(share_count):
        lifted = lax.dot_general(
            low_rank,
            first_parts[shift][:, rank:],
            (((1,), (1,)), ((), ())),
            preferred_element_type=jnp.float32,
        )
        shift_row = bias_blocks[position_feature[shift]].reshape(position_count * entry_count)
        columns = base_parts[shift].astype(jnp.float32)
        crossed = (columns * (lifted + shift_row[None, :]) + columns).astype(jnp.bfloat16)
        term = jnp.dot(crossed, second_parts[shift], preferred_element_type=jnp.float32)
        squeezed = term if squeezed is None else squeezed + term
    compressed = (squeezed + compress_bias[0][None, :]).astype(jnp.bfloat16)
    gathered = lax.all_to_all(compressed, "tower", split_axis=0, concat_axis=1, tiled=True)
    local_rows = gathered.shape[0]
    vector_count = gathered.shape[1] // entry_count
    vectors = gathered.reshape(local_rows, vector_count, entry_count)
    gram_matrix = jnp.einsum(
        "bie,bje->bij", vectors, vectors, preferred_element_type=jnp.float32
    ) * (1.0 / math.sqrt(entry_count))
    pair_terms = gram_matrix.reshape(local_rows, vector_count * vector_count)[
        :, pair_positions(vector_count)
    ]
    joined = jnp.concatenate([dense_vector.astype(jnp.float32), pair_terms], 1).astype(jnp.bfloat16)
    hidden_units = mlp_weight.shape[1]
    width_here = hidden_weight.shape[0]
    columns = lax.slice_in_dim(joined, 0, width_here, axis=1)
    hidden_sum = jnp.zeros((local_rows, hidden_units), jnp.float32) + jnp.dot(
        columns, hidden_weight, preferred_element_type=jnp.float32
    )
    return jax.nn.relu(hidden_sum + mlp_bias[None, :]).astype(jnp.bfloat16)


def solution(mesh):
    in_specs = (
        P("tower", "feat", "groups", None),
        P("tower", "feat", "groups", None),
        P("tower", None),
        P("tower", "feat", None),
        P("tower", "feat", None),
        P("tower", None),
        P("tower", "feat", None),
        P("tower", None),
        P(("groups", "feat", "tower"), None),
        P("tower", None),
        P(),
    )
    out_specs = P(("groups", "feat", "tower"), None)
    body = functools.partial(
        on_device, feat_count=mesh.shape["feat"], group_count=mesh.shape["groups"]
    )
    return jax.shard_map(body, mesh=mesh, in_specs=in_specs, out_specs=out_specs, check_vma=False)
```

profile of v0, /device:TPU:0, one launch (start us, length us, event | category | flops | bytes accessed | tf_op | source)
XLA Modules:
  0.0 243.4 jit_solution(15778819335520418898)
XLA Ops:
  6.5 2.0 fusion.30
  8.6 8.2 %copy.25 = bf16[1,4,1536,128]{3,1,0,2:T(4,128)(2,1)} copy(bf16[1,4,1536,128]{3,2,1,0:T(8,128)(2,1)S(1)} %copy-done.2) | data formatting | bytes 3145728 | tf_op args[0]
  16.8 6.3 %all-to-all-start = ((bf16[1,4,1536,128]{3,1,0,2:T(4,128)(2,1)}), bf16[1,4,1536,128]{3,1,0,2:T(4,128)(2,1)S(1)}, u32[]{:S(2)}, u32[]{:S(2)}) async-start(bf16[1,4,1536,128]{3,1,0,2:T(4,128)(2,1)} %copy.25), calls=%async_computation | async-start | bytes 3145728 | tf_op jit(solution)/shard_map/all_to_all | solution.py:75
  23.2 0.9 constant_dynamic-slice_fusion
  24.0 8.5 %copy.27 = bf16[1,4,1536,128]{3,1,0,2:T(4,128)(2,1)} copy(bf16[1,4,1536,128]{3,2,1,0:T(8,128)(2,1)} %param.15) | data formatting | bytes 3145728 | tf_op args[1]
  32.6 58.1 %all-to-all-done = bf16[1,4,1536,128]{3,1,0,2:T(4,128)(2,1)S(1)} async-done(((bf16[1,4,1536,128]{3,1,0,2:T(4,128)(2,1)}), bf16[1,4,1536,128]{3,1,0,2:T(4,128)(2,1)S(1)}, u32[]{:S(2)}, u32[]{:S(2)}) %all-to-all-start) | async-done | bytes 1572896 | tf_op jit(solution)/shard_map/all_to_all | solution.py:75
  90.7 4.6 %all-to-all-start.1 = ((bf16[1,4,1536,128]{3,1,0,2:T(4,128)(2,1)}), bf16[1,4,1536,128]{3,1,0,2:T(4,128)(2,1)}, u32[]{:S(2)}, u32[]{:S(2)}) async-start(bf16[1,4,1536,128]{3,1,0,2:T(4,128)(2,1)} %copy.27), calls=%async_computation.1 | async-start | bytes 3145728 | tf_op jit(solution)/shard_map/all_to_all | solution.py:76
  95.3 1.5 collective-permute-start
  96.9 69.6 %all-gather.7.cloned.1.call-done = bf16[1,2048,512]{2,1,0:T(8,128)(2,1)} async-done(((bf16[1,512,512]{2,1,0:T(8,128)(2,1)}), bf16[1,2048,512]{2,1,0:T(8,128)(2,1)}) %all-gather.7.cloned.1.call-update) | async-done | bytes 2097168 | tf_op jit(solution)/shard_map/all_gather | solution.py:30
  166.5 1.5 collective-permute-start.1
  168.6 0.6 gather_fusion.1
  169.1 1.8 copy.26
  170.9 2.1 copy.28
  173.0 1.0 convert_bitcast_fusion
  174.6 1.2 copy-done.11
  175.8 0.6 fusion.7
  176.4 1.8 fusion.18
  178.2 4.9 %fusion.28 = f32[384,512]{1,0:T(8,128)} fusion(bf16[384,256]{1,0:T(8,128)(2,1)S(1)} %fusion.18, f32[2048]{0:T(1024)S(1)} %bitcast.92, bf16[48,8,16,128]{3,2,1,0:T(8,128)(2,1)} %bitcast.83, bf16[2048,512]{1,0:T(8,128)(2,1)} %all-gather.5.cloned.1.call-done, bf16[1,2048,512]{2,1,0:T(8,128)(2,1)} %all-gather.7.cloned.1.call-done), kind=kOutput, calls=%fused_computation.33 | convolution fusion | flops 1211891712 | bytes 5709824 | tf_op jit(solution)/shard_map/dot_general | solution.py:109
  183.1 31.3 %collective-permute-done.1 = bf16[2048,512]{1,0:T(8,128)(2,1)} collective-permute-done((bf16[2048,512]{1,0:T(8,128)(2,1)}, bf16[2048,512]{1,0:T(8,128)(2,1)}, u32[]{:S(2)}, u32[]{:S(2)}) %collective-permute-start.1) | collective-permute-done | bytes 2097184 | tf_op jit(solution)/shard_map/ppermute | solution.py:34
  214.4 4.5 %fusion.12 = bf16[384,512]{1,0:T(8,128)(2,1)} fusion(f32[384,512]{1,0:T(8,128)} %fusion.28, bf16[2048,512]{1,0:T(8,128)(2,1)} %collective-permute-done.1, bf16[384,256]{1,0:T(8,128)(2,1)S(1)} %fusion.18, f32[2048]{0:T(1024)S(1)} %bitcast.91, bf16[48,8,16,128]{3,2,1,0:T(8,128)(2,1)S(1)} %bitcast.81, bf16[2048,512]{1,0:T(8,128)(2,1)} %collective-permute-done, ...), kind=kOutput, calls=%fused_computation.21 | convolution fusion | flops 1212481536 | bytes 6105088 | tf_op jit(solution)/shard_map/dot_general | solution.py:109
  218.9 3.5 %all-to-all-start.2 = ((bf16[4,96,512]{2,1,0:T(8,128)(2,1)}), bf16[4,96,512]{2,1,0:T(8,128)(2,1)S(1)}, u32[]{:S(2)}, u32[]{:S(2)}) async-start(bf16[4,96,512]{2,1,0:T(8,128)(2,1)} %bitcast.24), calls=%async_computation.2 | async-start | bytes 786432 | tf_op jit(solution)/shard_map/all_to_all | solution.py:112
  222.4 11.0 %all-gather.1 = bf16[4,62,1024]{2,1,0:T(8,128)(2,1)S(1)} all-gather(bf16[1,62,1024]{2,1,0:T(8,128)(2,1)S(1)} %bitcast.89), channel_id=1, replica_groups=mesh['groups'=2,'feat'=4,'tower'=4] {'tower'}, dimensions={0}, use_global_device_ids=true | all-gather | bytes 634880 | tf_op jit(solution)/shard_map/all_gather | solution.py:79
  234.8 0.7 gather_fusion.2
  235.6 0.9 fusion.17
  (45 shorter events, 2.6 us)
Async XLA Ops:
  6.5 16.6 %copy-start = (bf16[1,1024,512]{2,1,0:T(8,128)(2,1)S(1)}, bf16[1,1024,512]{2,1,0:T(8,128)(2,1)}, u32[]{:S(2)}) copy-start(bf16[1,1024,512]{2,1,0:T(8,128)(2,1)} %param.20) | copy-start | bytes 3145732
  6.5 2.1 copy-start.2
  6.5 88.8 %all-gather.5.cloned.1.call-start = ((), (), s32[]{:S(2)}) async-start(), calls=%async_computation.3 | async-start | bytes 2621440 | tf_op jit(solution)/shard_map/all_gather | solution.py:30
  16.8 73.9 %all-to-all-start = ((bf16[1,4,1536,128]{3,1,0,2:T(4,128)(2,1)}), bf16[1,4,1536,128]{3,1,0,2:T(4,128)(2,1)S(1)}, u32[]{:S(2)}, u32[]{:S(2)}) async-start(bf16[1,4,1536,128]{3,1,0,2:T(4,128)(2,1)} %copy.25), calls=%async_computation | async-start | bytes 3145728 | tf_op jit(solution)/shard_map/all_to_all | solution.py:75
  23.2 143.3 %all-gather.7.cloned.1.call-start = ((), (), s32[]{:S(2)}) async-start(), calls=%async_computation.4 | async-start | bytes 2621440 | tf_op jit(solution)/shard_map/all_gather | solution.py:30
  32.6 135.4 %copy-start.9 = (s32[2,2,16]{2,1,0:T(2,128)S(1)}, s32[2,2,16]{2,1,0:T(2,128)}, u32[]{:S(2)}) copy-start(s32[2,2,16]{2,1,0:T(2,128)} %constant.31.clone) | copy-start | bytes 772
  32.6 135.4 %copy-start.4 = (f32[1,4096]{1,0:T(1,128)S(1)}, f32[1,4096]{1,0:T(1,128)}, u32[]{:S(2)}) copy-start(f32[1,4096]{1,0:T(1,128)} %param.19) | copy-start | bytes 49156
  90.7 80.2 %all-to-all-start.1 = ((bf16[1,4,1536,128]{3,1,0,2:T(4,128)(2,1)}), bf16[1,4,1536,128]{3,1,0,2:T(4,128)(2,1)}, u32[]{:S(2)}, u32[]{:S(2)}) async-start(bf16[1,4,1536,128]{3,1,0,2:T(4,128)(2,1)} %copy.27), calls=%async_computation.1 | async-start | bytes 3145728 | tf_op jit(solution)/shard_map/all_to_all | solution.py:76
  95.3 81.0 %collective-permute-start = (bf16[2048,512]{1,0:T(8,128)(2,1)}, bf16[2048,512]{1,0:T(8,128)(2,1)}, u32[]{:S(2)}, u32[]{:S(2)}) collective-permute-start(bf16[2048,512]{1,0:T(8,128)(2,1)} %all-gather.5.cloned.1.call-done), channel_id=1, source_target_pairs={{0,16},{16,0},{1,17},{17,1},{2,18},{18,2},{3,19},{19,3},{4,20},{20... | collective-permute-start | bytes 6291464 | tf_op jit(solution)/shard_map/ppermute | solution.py:34
  166.5 47.9 %collective-permute-start.1 = (bf16[2048,512]{1,0:T(8,128)(2,1)}, bf16[2048,512]{1,0:T(8,128)(2,1)}, u32[]{:S(2)}, u32[]{:S(2)}) collective-permute-start(bf16[2048,512]{1,0:T(8,128)(2,1)} %bitcast.94), channel_id=1, source_target_pairs={{0,16},{16,0},{1,17},{17,1},{2,18},{18,2},{3,19},{19,3},{4,20},{20... | collective-permute-start | bytes 6291464 | tf_op jit(solution)/shard_map/ppermute | solution.py:34
  170.9 2.1 copy-start.1
  170.9 2.1 copy-start.8
  174.0 1.7 copy-start.11
  174.6 1.8 copy-start.3
  178.2 36.2 %copy-start.12 = (f32[1,512]{1,0:T(1,128)S(1)}, f32[1,512]{1,0:T(1,128)}, u32[]{:S(2)}) copy-start(f32[1,512]{1,0:T(1,128)} %param.21) | copy-start | bytes 6148
  214.4 8.0 %copy-start.10 = (s32[120]{0:T(128)S(1)}, s32[120]{0:T(128)}, u32[]{:S(2)}) copy-start(s32[120]{0:T(128)} %constant.44) | copy-start | bytes 1444
  214.4 8.0 %copy-start.5 = (bf16[62,1024]{1,0:T(8,128)(2,1)S(1)}, bf16[62,1024]{1,0:T(8,128)(2,1)}, u32[]{:S(2)}) copy-start(bf16[62,1024]{1,0:T(8,128)(2,1)} %param.23) | copy-start | bytes 380932
  218.9 14.7 %all-to-all-start.2 = ((bf16[4,96,512]{2,1,0:T(8,128)(2,1)}), bf16[4,96,512]{2,1,0:T(8,128)(2,1)S(1)}, u32[]{:S(2)}, u32[]{:S(2)}) async-start(bf16[4,96,512]{2,1,0:T(8,128)(2,1)} %bitcast.24), calls=%async_computation.2 | async-start | bytes 786432 | tf_op jit(solution)/shard_map/all_to_all | solution.py:112
  233.5 2.1 copy-start.6
  233.5 2.1 copy-start.7
Sparse Core Ops, SparseCore 0:
  8.9 80.4 all-gather.4
  91.0 75.4 all-gather.6
where the time goes:
time: 244 us; the launch traced here: 243 us
  waiting for transfers between devices  159 us (65%)
  local copies, waits for them, and re-layouts  26.1 us (11%)
  starting transfers between devices  17.4 us (7%)
  matrix products  14.1 us (6%)
  between operations  13.6 us (6%)
  blocking collectives  11 us (5%)
    all_gather x2, waiting for transfers between devices, gather_rows(): own = lax.all_gather(part, 'feat', axis=0, tiled=True)  69.6 us
    all_to_all x1, waiting for transfers between devices, on_device(): lax.all_to_all(pooled_first, 'feat', split_axis=2, concat_axis=1, tiled=T...  58.1 us
    ppermute x2, waiting for transfers between devices, gather_rows(): received.append(lax.ppermute(own, 'groups', pairs))  31.3 us
    unnamed x29, local copies, waits for them, and re-layouts  18.1 us
    all_gather x1, blocking collectives, on_device(): hidden_weight = lax.all_gather(mlp_weight, 'tower', axis=0, tiled=True)  11 us
    dot_general x2, matrix products, on_device(): jnp.dot(crossed, second_parts[shift], preferred_element_type=jnp.float32)  9.42 us
    all_to_all x1, starting transfers between devices, on_device(): lax.all_to_all(pooled_first, 'feat', split_axis=2, concat_axis=1, tiled=T...  6.32 us
  transfers between devices with their start and end apart: 7, of which 3 were waited for; matrix products, arithmetic and copies ran while one was open for 13% of the time, Pallas kernels for 0%

commit v1 on v0

--- a/solution.py
+++ b/solution.py
@@ -73,7 +73,12 @@
     second_parts = gather_rows(second_here, share_count)
     group_one, group_two = (
         lax.all_to_all(pooled_first, "feat", split_axis=2, concat_axis=1, tiled=True),
-        lax.all_to_all(pooled_second, "feat", split_axis=2, concat_axis=1, tiled=True),
+        jnp.concatenate(
+            lax.all_to_all(
+                jnp.stack(jnp.split(pooled_second, lax.axis_size("feat"), axis=2)), "feat", 0, 0
+            ),
+            axis=1,
+        ),
     )
     mlp_weight, group_one = lax.optimization_barrier((mlp_weight, group_one))
     hidden_weight = lax.all_gather(mlp_weight, "tower", axis=0, tiled=True)

time: 244 us -> 244 us (level)
  local copies, waits for them, and re-layouts: 26.1 us -> 19.7 us
  waiting for transfers between devices: 159 us -> 164 us
    unnamed x29 -> x28, local copies, waits for them, and re-layouts: 18.1 us -> 9.61 us
    all_to_all x1, waiting for transfers between devices: 58.1 us -> 63.8 us  [on_device(): lax.all_to_all(pooled_first, 'feat', split_axis=2, concat_axis=1, tiled=T...]
  transfers between devices with their start and end apart: 7 -> 7, of which waited for: 3 -> 3; matrix products, arithmetic and copies ran while one was open for 13% -> 11% of each run, Pallas kernels for 0% -> 0%
where the time goes in v1:
time: 244 us; the launch traced here: 243 us
  waiting for transfers between devices  164 us (67%)
  local copies, waits for them, and re-layouts  19.7 us (8%)
  starting transfers between devices  17.4 us (7%)
  matrix products  14 us (6%)
  between operations  13.6 us (6%)
  blocking collectives  11 us (5%)
  other arithmetic  3.43 us (1%)
    all_gather x2, waiting for transfers between devices, gather_rows(): own = lax.all_gather(part, 'feat', axis=0, tiled=True)  69.6 us
    all_to_all x1, waiting for transfers between devices, on_device(): lax.all_to_all(pooled_first, 'feat', split_axis=2, concat_axis=1, tiled=T...  63.8 us
    ppermute x2, waiting for transfers between devices, gather_rows(): received.append(lax.ppermute(own, 'groups', pairs))  30.7 us
    all_gather x1, blocking collectives, on_device(): hidden_weight = lax.all_gather(mlp_weight, 'tower', axis=0, tiled=True)  11 us
    unnamed x28, local copies, waits for them, and re-layouts  9.61 us
    dot_general x2, matrix products, on_device(): jnp.dot(crossed, second_parts[shift], preferred_element_type=jnp.float32)  9.4 us
    all_to_all x1, starting transfers between devices, on_device(): lax.all_to_all(pooled_first, 'feat', split_axis=2, concat_axis=1, tiled=T...  6.32 us
  transfers between devices with their start and end apart: 7, of which 3 were waited for; matrix products, arithmetic and copies ran while one was open for 11% of the time, Pallas kernels for 0%

profile of v1, /device:TPU:0, one launch (start us, length us, event | category | flops | bytes accessed | tf_op | source)
XLA Modules:
  0.0 243.3 jit_solution(237282516728330481)
XLA Ops:
  6.5 2.0 fusion.30
  8.6 8.3 %copy.25 = bf16[1,4,1536,128]{3,1,0,2:T(4,128)(2,1)} copy(bf16[1,4,1536,128]{3,2,1,0:T(8,128)(2,1)S(1)} %copy-done.2) | data formatting | bytes 3145728 | tf_op args[0]
  16.9 6.3 %all-to-all-start = ((bf16[1,4,1536,128]{3,1,0,2:T(4,128)(2,1)}), bf16[1,4,1536,128]{3,1,0,2:T(4,128)(2,1)S(1)}, u32[]{:S(2)}, u32[]{:S(2)}) async-start(bf16[1,4,1536,128]{3,1,0,2:T(4,128)(2,1)} %copy.25), calls=%async_computation | async-start | bytes 3145728 | tf_op jit(solution)/shard_map/all_to_all | solution.py:75
  23.2 0.9 constant_dynamic-slice_fusion
  24.1 1.5 slice_bitcast_fusion.3
  25.5 1.4 pad_maximum_fusion
  26.9 63.8 %all-to-all-done = bf16[1,4,1536,128]{3,1,0,2:T(4,128)(2,1)S(1)} async-done(((bf16[1,4,1536,128]{3,1,0,2:T(4,128)(2,1)}), bf16[1,4,1536,128]{3,1,0,2:T(4,128)(2,1)S(1)}, u32[]{:S(2)}, u32[]{:S(2)}) %all-to-all-start) | async-done | bytes 1572896 | tf_op jit(solution)/shard_map/all_to_all | solution.py:75
  90.7 4.5 %all-to-all-start.1 = ((bf16[4,1,4,384,128]{4,3,2,1,0:T(8,128)(2,1)}), bf16[4,1,4,384,128]{4,3,2,1,0:T(8,128)(2,1)}, u32[]{:S(2)}, u32[]{:S(2)}) async-start(bf16[4,1,4,384,128]{4,3,2,1,0:T(8,128)(2,1)} %pad_maximum_fusion), calls=%async_computation.1 | async-start | bytes 3145728 | tf_op jit(solution)/shard_map/all_to_all | solution.py:77
  95.3 1.5 collective-permute-start
  96.8 69.6 %all-gather.7.cloned.1.call-done = bf16[1,2048,512]{2,1,0:T(8,128)(2,1)} async-done(((bf16[1,512,512]{2,1,0:T(8,128)(2,1)}), bf16[1,2048,512]{2,1,0:T(8,128)(2,1)}) %all-gather.7.cloned.1.call-update) | async-done | bytes 2097168 | tf_op jit(solution)/shard_map/all_gather | solution.py:30
  166.5 1.5 collective-permute-start.1
  169.1 1.8 copy.26
  170.9 2.7 %copy.27 = bf16[4,1,4,384,128]{4,2,0,3,1:T(4,128)(2,1)S(1)} copy(bf16[4,1,4,384,128]{4,3,2,1,0:T(8,128)(2,1)} %all-to-all-done.1) | data formatting | bytes 3145728 | tf_op jit(solution)/shard_map/all_to_all | solution.py:77
  173.7 1.0 convert_bitcast_fusion
  175.2 1.2 copy-done.11
  176.4 0.6 fusion.7
  177.0 1.8 fusion.18
  178.8 4.9 %fusion.28 = f32[384,512]{1,0:T(8,128)} fusion(bf16[384,256]{1,0:T(8,128)(2,1)S(1)} %fusion.18, f32[2048]{0:T(1024)S(1)} %bitcast.97, bf16[48,8,16,128]{3,2,1,0:T(8,128)(2,1)} %bitcast.88, bf16[2048,512]{1,0:T(8,128)(2,1)} %all-gather.5.cloned.1.call-done, bf16[1,2048,512]{2,1,0:T(8,128)(2,1)} %all-gather.7.cloned.1.call-done), kind=kOutput, calls=%fused_computation.34 | convolution fusion | flops 1211891712 | bytes 5709824 | tf_op jit(solution)/shard_map/dot_general | solution.py:114
  183.7 30.7 %collective-permute-done.1 = bf16[2048,512]{1,0:T(8,128)(2,1)} collective-permute-done((bf16[2048,512]{1,0:T(8,128)(2,1)}, bf16[2048,512]{1,0:T(8,128)(2,1)}, u32[]{:S(2)}, u32[]{:S(2)}) %collective-permute-start.1) | collective-permute-done | bytes 2097184 | tf_op jit(solution)/shard_map/ppermute | solution.py:34
  214.4 4.5 %fusion.12 = bf16[384,512]{1,0:T(8,128)(2,1)} fusion(f32[384,512]{1,0:T(8,128)} %fusion.28, bf16[2048,512]{1,0:T(8,128)(2,1)} %collective-permute-done.1, bf16[384,256]{1,0:T(8,128)(2,1)S(1)} %fusion.18, f32[2048]{0:T(1024)S(1)} %bitcast.96, bf16[48,8,16,128]{3,2,1,0:T(8,128)(2,1)S(1)} %bitcast.86, bf16[2048,512]{1,0:T(8,128)(2,1)} %collective-permute-done, ...), kind=kOutput, calls=%fused_computation.22 | convolution fusion | flops 1212481536 | bytes 6105088 | tf_op jit(solution)/shard_map/dot_general | solution.py:114
  218.9 3.5 %all-to-all-start.2 = ((bf16[4,96,512]{2,1,0:T(8,128)(2,1)}), bf16[4,96,512]{2,1,0:T(8,128)(2,1)S(1)}, u32[]{:S(2)}, u32[]{:S(2)}) async-start(bf16[4,96,512]{2,1,0:T(8,128)(2,1)} %bitcast.26), calls=%async_computation.2 | async-start | bytes 786432 | tf_op jit(solution)/shard_map/all_to_all | solution.py:117
  222.4 11.0 %all-gather.1 = bf16[4,62,1024]{2,1,0:T(8,128)(2,1)S(1)} all-gather(bf16[1,62,1024]{2,1,0:T(8,128)(2,1)S(1)} %bitcast.94), channel_id=1, replica_groups=mesh['groups'=2,'feat'=4,'tower'=4] {'tower'}, dimensions={0}, use_global_device_ids=true | all-gather | bytes 634880 | tf_op jit(solution)/shard_map/all_gather | solution.py:84
  234.8 0.7 gather_fusion.2
  235.6 0.9 fusion.17
  (46 shorter events, 3.2 us)
Async XLA Ops:
  6.5 16.6 %copy-start = (bf16[1,1024,512]{2,1,0:T(8,128)(2,1)S(1)}, bf16[1,1024,512]{2,1,0:T(8,128)(2,1)}, u32[]{:S(2)}) copy-start(bf16[1,1024,512]{2,1,0:T(8,128)(2,1)} %param.20) | copy-start | bytes 3145732
  6.5 2.1 copy-start.2
  6.5 88.7 %all-gather.5.cloned.1.call-start = ((), (), s32[]{:S(2)}) async-start(), calls=%async_computation.3 | async-start | bytes 2621440 | tf_op jit(solution)/shard_map/all_gather | solution.py:30
  16.9 73.9 %all-to-all-start = ((bf16[1,4,1536,128]{3,1,0,2:T(4,128)(2,1)}), bf16[1,4,1536,128]{3,1,0,2:T(4,128)(2,1)S(1)}, u32[]{:S(2)}, u32[]{:S(2)}) async-start(bf16[1,4,1536,128]{3,1,0,2:T(4,128)(2,1)} %copy.25), calls=%async_computation | async-start | bytes 3145728 | tf_op jit(solution)/shard_map/all_to_all | solution.py:75
  23.2 143.3 %all-gather.7.cloned.1.call-start = ((), (), s32[]{:S(2)}) async-start(), calls=%async_computation.4 | async-start | bytes 2621440 | tf_op jit(solution)/shard_map/all_gather | solution.py:30
  26.9 141.0 %copy-start.9 = (s32[2,2,16]{2,1,0:T(2,128)S(1)}, s32[2,2,16]{2,1,0:T(2,128)}, u32[]{:S(2)}) copy-start(s32[2,2,16]{2,1,0:T(2,128)} %constant.31.clone) | copy-start | bytes 772
  26.9 141.0 %copy-start.4 = (f32[1,4096]{1,0:T(1,128)S(1)}, f32[1,4096]{1,0:T(1,128)}, u32[]{:S(2)}) copy-start(f32[1,4096]{1,0:T(1,128)} %param.19) | copy-start | bytes 49156
  90.7 80.2 %all-to-all-start.1 = ((bf16[4,1,4,384,128]{4,3,2,1,0:T(8,128)(2,1)}), bf16[4,1,4,384,128]{4,3,2,1,0:T(8,128)(2,1)}, u32[]{:S(2)}, u32[]{:S(2)}) async-start(bf16[4,1,4,384,128]{4,3,2,1,0:T(8,128)(2,1)} %pad_maximum_fusion), calls=%async_computation.1 | async-start | bytes 3145728 | tf_op jit(solution)/shard_map/all_to_all | solution.py:77
  95.3 81.7 %collective-permute-start = (bf16[2048,512]{1,0:T(8,128)(2,1)}, bf16[2048,512]{1,0:T(8,128)(2,1)}, u32[]{:S(2)}, u32[]{:S(2)}) collective-permute-start(bf16[2048,512]{1,0:T(8,128)(2,1)} %all-gather.5.cloned.1.call-done), channel_id=1, source_target_pairs={{0,16},{16,0},{1,17},{17,1},{2,18},{18,2},{3,19},{19,3},{4,20},{20... | collective-permute-start | bytes 6291464 | tf_op jit(solution)/shard_map/ppermute | solution.py:34
  166.5 47.9 %collective-permute-start.1 = (bf16[2048,512]{1,0:T(8,128)(2,1)}, bf16[2048,512]{1,0:T(8,128)(2,1)}, u32[]{:S(2)}, u32[]{:S(2)}) collective-permute-start(bf16[2048,512]{1,0:T(8,128)(2,1)} %bitcast.99), channel_id=1, source_target_pairs={{0,16},{16,0},{1,17},{17,1},{2,18},{18,2},{3,19},{19,3},{4,20},{20... | collective-permute-start | bytes 6291464 | tf_op jit(solution)/shard_map/ppermute | solution.py:34
  170.9 2.8 %copy-start.1 = (bf16[1,4,4,384,128]{4,1,2,3,0:T(4,128)(2,1)S(1)}, bf16[1,4,4,384,128]{4,1,2,3,0:T(4,128)(2,1)}, u32[]{:S(2)}) copy-start(bf16[1,4,4,384,128]{4,1,2,3,0:T(4,128)(2,1)} %copy.26) | copy-start | bytes 4718596
  170.9 2.8 %copy-start.8 = (s32[1,32]{1,0:T(1,128)S(1)}, s32[1,32]{1,0:T(1,128)}, u32[]{:S(2)}) copy-start(s32[1,32]{1,0:T(1,128)} %param.16) | copy-start | bytes 388
  174.7 1.7 copy-start.11
  175.2 1.8 copy-start.3
  178.8 35.6 %copy-start.12 = (f32[1,512]{1,0:T(1,128)S(1)}, f32[1,512]{1,0:T(1,128)}, u32[]{:S(2)}) copy-start(f32[1,512]{1,0:T(1,128)} %param.21) | copy-start | bytes 6148
  214.4 8.0 %copy-start.10 = (s32[120]{0:T(128)S(1)}, s32[120]{0:T(128)}, u32[]{:S(2)}) copy-start(s32[120]{0:T(128)} %constant.44) | copy-start | bytes 1444
  214.4 8.0 %copy-start.5 = (bf16[62,1024]{1,0:T(8,128)(2,1)S(1)}, bf16[62,1024]{1,0:T(8,128)(2,1)}, u32[]{:S(2)}) copy-start(bf16[62,1024]{1,0:T(8,128)(2,1)} %param.23) | copy-start | bytes 380932
  218.9 14.7 %all-to-all-start.2 = ((bf16[4,96,512]{2,1,0:T(8,128)(2,1)}), bf16[4,96,512]{2,1,0:T(8,128)(2,1)S(1)}, u32[]{:S(2)}, u32[]{:S(2)}) async-start(bf16[4,96,512]{2,1,0:T(8,128)(2,1)} %bitcast.26), calls=%async_computation.2 | async-start | bytes 786432 | tf_op jit(solution)/shard_map/all_to_all | solution.py:117
  233.4 2.1 copy-start.6
  233.4 2.1 copy-start.7
Sparse Core Ops, SparseCore 0:
  8.9 80.4 all-gather.4
  91.0 75.4 all-gather.6
